TPU v7x, 512 devices: a whole 4x4x16 slice. The times are simulated.
512 devices in a mesh: row: 16 (over z), col: 4 (over x_hi, core), depth: 8 (over y, x_lo).
Axes of the slice: x: 4 (x_hi: 2, x_lo: 2; x = x_hi * 2 + x_lo), y: 4, z: 16, core: 2. Of those that a mesh axis runs over, the one named last changes fastest.
Arguments:
- ks_matrix: bfloat16 [4096, 16384], P('col', ('row', 'depth')), may hold values from -6 to 6
- sign_matrix: bfloat16 [16, 8, 128, 12288], P('col', 'depth', None, 'row'), may hold values from -0.046875 to 0.046875
- ks_mask: int32 [32, 128], P('col', ('row', 'depth')), may hold values 0 or 1
- sign_mask: int32 [16, 8, 1, 96], P('col', 'depth', None, 'row'), may hold values 0 or 1
- product_mask: int32 [32, 96], P('col', 'row'), may hold values 0 or 1
- row_order: int32 [4, 8], P('col'), may hold values from 0 to 7, each once within a row
Outputs:
- next_matrix: bfloat16 [4096, 12288], P(('col', 'depth'), 'row')
Inputs may be any that keep to these rules, and one draw needn't show every extreme that they name: Each row of row_order names every number of 0 to 7 once.
All inputs are finite; a program needn't handle non-finite values. No bound on the sum of `ks_mask` or of `sign_mask` or of `product_mask` on one device may be relied on, other than what follows from the above.
Results may differ from a plain program's by a relative error of at most 0.001.
Values may be sent and summed in bfloat16 or wider, within the bound.
No kernel may reach another device: no remote copies, remote signals or barrier semaphores. Data moves between devices by JAX's collectives and lax.ppermute only.
A program may use at most 64 MiB of HBM per device.

v0:
```python
import jax
import jax.numpy as jnp
from jax import lax
from jax.sharding import PartitionSpec as P

BS = 128


def from_behind(block, axis, distance):
    devices = range(lax.axis_size(axis))
    route = [((i - distance) % len(devices), i) for i in devices]
    return lax.ppermute(block, axis, route)


def per_device(ks_matrix, sign_matrix, ks_mask, sign_mask, product_mask, row_order):
    row_blocks, inner_blocks = ks_mask.shape
    local_groups = sign_mask.shape[0]
    sign_inner = sign_mask.shape[2]
    col_blocks = sign_mask.shape[3]
    ks_panel = (
        ks_matrix.reshape(row_blocks, BS, inner_blocks, BS)
        * ks_mask.astype(jnp.bfloat16)[:, None, :, None]
    )
    ks_panel = ks_panel.reshape(row_blocks * BS, inner_blocks * BS)
    sign_kept = sign_matrix.reshape(local_groups, sign_inner, BS, col_blocks, BS)
    sign_kept = sign_kept * sign_mask.astype(jnp.bfloat16).reshape(
        local_groups, sign_inner, 1, col_blocks, 1
    )
    sign_kept = sign_kept.reshape(local_groups, 1, sign_inner * BS, col_blocks * BS)
    sign_whole = lax.all_gather(sign_kept, "col", axis=0, tiled=True)
    row_count = lax.axis_size("row")
    start_sum = jnp.zeros((row_blocks * BS, col_blocks * BS), jnp.float32)
    row_index = lax.axis_index("row")

    def advance(step, carry):
        running, moving = carry
        source = (row_index - step) % row_count
        sign_piece = lax.dynamic_index_in_dim(sign_whole, source, 0, keepdims=False)[0]
        running = running + jnp.dot(moving, sign_piece, preferred_element_type=jnp.float32)
        moving = from_behind(moving, "row", 1)
        return (running, moving)

    running, moving = lax.fori_loop(0, row_count - 1, advance, (start_sum, ks_panel))
    final_source = (row_index - row_count + 1) % row_count
    final_piece = lax.dynamic_index_in_dim(sign_whole, final_source, 0, keepdims=False)[0]
    running = running + jnp.dot(moving, final_piece, preferred_element_type=jnp.float32)
    depth_count = lax.axis_size("depth")
    part_rows = row_blocks // depth_count
    filtered = (
        running.reshape(row_blocks, BS, col_blocks, BS)
        * product_mask.astype(jnp.float32)[:, None, :, None]
    )
    local_order = row_order[0]
    summed = lax.psum(filtered, "depth")
    own_rows = lax.dynamic_slice_in_dim(
        local_order, lax.axis_index("depth") * part_rows, part_rows, 0
    )
    picked = jnp.take(summed, own_rows, axis=0)
    return picked.reshape(part_rows * BS, col_blocks * BS).astype(jnp.bfloat16)


def solution(mesh):
    in_specs = (
        P("col", ("row", "depth")),
        P("col", "depth", None, "row"),
        P("col", ("row", "depth")),
        P("col", "depth", None, "row"),
        P("col", "row"),
        P("col", None),
    )
    out_specs = P(("col", "depth"), "row")
    return jax.shard_map(
        per_device, mesh=mesh, in_specs=in_specs, out_specs=out_specs, check_vma=False
    )
```

profile of v0, /device:TPU:4, one launch (start us, length us, event | category | flops | bytes accessed | tf_op | source)
XLA Modules:
  0.0 356.8 jit_solution(18374426383536028386)
XLA Ops:
  7.3 2.1 broadcast_multiply_fusion.1
  13.5 1.9 broadcast_multiply_fusion.2
  15.4 36.3 %all-gather.2.cloned.1.call-done = bf16[16,1,128,768]{3,2,1,0:T(8,128)(2,1)} async-done(((bf16[4,1,128,768]{3,2,1,0:T(8,128)(2,1)}), bf16[16,1,128,768]{3,2,1,0:T(8,128)(2,1)}) %all-gather.2.cloned.1.call-update) | async-done | bytes 3145744 | tf_op jit(solution)/shard_map/all_gather | solution.py:30
  51.6 171.1 %while.19 = (s32[]{:T(128)}, f32[1024,768]{0,1:T(8,128)S(1)}, bf16[1024,128]{1,0:T(8,128)(2,1)}, s32[]{:T(128)}, bf16[16,1,128,768]{3,2,1,0:T(8,128)(2,1)}, /*index=5*/s32[]{:T(128)}, s32[]{:T(128)}, s32[]{:T(128)}, s32[]{:T(128)}) while((s32[]{:T(128)}, f32[1024,768]{0,1:T(8,128)S(1)}, bf16[1024,128]{1,0:T(8,128)(2,1)}, ...), condition=%wide.region_1.2_spmd.clone, body=%wide.region_0.1_spmd.clone.sunk | while | flops 202899472 | bytes 8323374 | solution.py:43
  52.6 3.7 %collective-permute-start = (bf16[1024,128]{1,0:T(8,128)(2,1)S(1)}, bf16[1024,128]{1,0:T(8,128)(2,1)}, u32[]{:S(2)}, u32[]{:S(2)}) collective-permute-start(bf16[1024,128]{1,0:T(8,128)(2,1)S(1)} %copy.29), channel_id=1, source_target_pairs={{480,0},{0,32},{32,64},{64,96},{96,128},{128,160},{160,192},{192,2... | collective-permute-start | bytes 786440 | tf_op jit(solution)/shard_map/while/body/eval_jaxpr/ppermute | solution.py:12
  56.3 1.9 bitcast_add_fusion.2
  58.2 7.4 %collective-permute-done = bf16[1024,128]{1,0:T(8,128)(2,1)} collective-permute-done((bf16[1024,128]{1,0:T(8,128)(2,1)S(1)}, bf16[1024,128]{1,0:T(8,128)(2,1)}, u32[]{:S(2)}, u32[]{:S(2)}) %collective-permute-start) | collective-permute-done | bytes 262176 | tf_op jit(solution)/shard_map/while/body/eval_jaxpr/ppermute | solution.py:12
  65.6 1.0 copy.29
  66.5 1.9 collective-permute-start
  68.5 1.9 bitcast_add_fusion.2
  70.3 7.3 %collective-permute-done = bf16[1024,128]{1,0:T(8,128)(2,1)} collective-permute-done((bf16[1024,128]{1,0:T(8,128)(2,1)S(1)}, bf16[1024,128]{1,0:T(8,128)(2,1)}, u32[]{:S(2)}, u32[]{:S(2)}) %collective-permute-start) | collective-permute-done | bytes 262176 | tf_op jit(solution)/shard_map/while/body/eval_jaxpr/ppermute | solution.py:12
  77.7 1.0 copy.29
  78.6 1.9 collective-permute-start
  80.6 1.9 bitcast_add_fusion.2
  82.4 6.5 %collective-permute-done = bf16[1024,128]{1,0:T(8,128)(2,1)} collective-permute-done((bf16[1024,128]{1,0:T(8,128)(2,1)S(1)}, bf16[1024,128]{1,0:T(8,128)(2,1)}, u32[]{:S(2)}, u32[]{:S(2)}) %collective-permute-start) | collective-permute-done | bytes 262176 | tf_op jit(solution)/shard_map/while/body/eval_jaxpr/ppermute | solution.py:12
  88.9 1.0 copy.29
  89.9 1.9 collective-permute-start
  91.8 1.9 bitcast_add_fusion.2
  93.7 5.7 %collective-permute-done = bf16[1024,128]{1,0:T(8,128)(2,1)} collective-permute-done((bf16[1024,128]{1,0:T(8,128)(2,1)S(1)}, bf16[1024,128]{1,0:T(8,128)(2,1)}, u32[]{:S(2)}, u32[]{:S(2)}) %collective-permute-start) | collective-permute-done | bytes 262176 | tf_op jit(solution)/shard_map/while/body/eval_jaxpr/ppermute | solution.py:12
  99.4 1.0 copy.29
  100.4 1.9 collective-permute-start
  102.3 1.9 bitcast_add_fusion.2
  104.2 5.7 %collective-permute-done = bf16[1024,128]{1,0:T(8,128)(2,1)} collective-permute-done((bf16[1024,128]{1,0:T(8,128)(2,1)S(1)}, bf16[1024,128]{1,0:T(8,128)(2,1)}, u32[]{:S(2)}, u32[]{:S(2)}) %collective-permute-start) | collective-permute-done | bytes 262176 | tf_op jit(solution)/shard_map/while/body/eval_jaxpr/ppermute | solution.py:12
  109.9 1.0 copy.29
  110.9 1.9 collective-permute-start
  112.8 1.9 bitcast_add_fusion.2
  114.7 5.7 %collective-permute-done = bf16[1024,128]{1,0:T(8,128)(2,1)} collective-permute-done((bf16[1024,128]{1,0:T(8,128)(2,1)S(1)}, bf16[1024,128]{1,0:T(8,128)(2,1)}, u32[]{:S(2)}, u32[]{:S(2)}) %collective-permute-start) | collective-permute-done | bytes 262176 | tf_op jit(solution)/shard_map/while/body/eval_jaxpr/ppermute | solution.py:12
  120.5 1.0 copy.29
  121.4 1.9 collective-permute-start
  123.4 1.9 bitcast_add_fusion.2
  125.2 5.7 %collective-permute-done = bf16[1024,128]{1,0:T(8,128)(2,1)} collective-permute-done((bf16[1024,128]{1,0:T(8,128)(2,1)S(1)}, bf16[1024,128]{1,0:T(8,128)(2,1)}, u32[]{:S(2)}, u32[]{:S(2)}) %collective-permute-start) | collective-permute-done | bytes 262176 | tf_op jit(solution)/shard_map/while/body/eval_jaxpr/ppermute | solution.py:12
  131.0 1.0 copy.29
  131.9 1.9 collective-permute-start
  133.9 1.9 bitcast_add_fusion.2
  135.8 6.7 %collective-permute-done = bf16[1024,128]{1,0:T(8,128)(2,1)} collective-permute-done((bf16[1024,128]{1,0:T(8,128)(2,1)S(1)}, bf16[1024,128]{1,0:T(8,128)(2,1)}, u32[]{:S(2)}, u32[]{:S(2)}) %collective-permute-start) | collective-permute-done | bytes 262176 | tf_op jit(solution)/shard_map/while/body/eval_jaxpr/ppermute | solution.py:12
  143.5 1.9 collective-permute-start
  145.4 1.9 bitcast_add_fusion.2
  147.3 7.9 %collective-permute-done = bf16[1024,128]{1,0:T(8,128)(2,1)} collective-permute-done((bf16[1024,128]{1,0:T(8,128)(2,1)S(1)}, bf16[1024,128]{1,0:T(8,128)(2,1)}, u32[]{:S(2)}, u32[]{:S(2)}) %collective-permute-start) | collective-permute-done | bytes 262176 | tf_op jit(solution)/shard_map/while/body/eval_jaxpr/ppermute | solution.py:12
  156.2 1.9 collective-permute-start
  158.1 1.9 bitcast_add_fusion.2
  160.0 8.0 %collective-permute-done = bf16[1024,128]{1,0:T(8,128)(2,1)} collective-permute-done((bf16[1024,128]{1,0:T(8,128)(2,1)S(1)}, bf16[1024,128]{1,0:T(8,128)(2,1)}, u32[]{:S(2)}, u32[]{:S(2)}) %collective-permute-start) | collective-permute-done | bytes 262176 | tf_op jit(solution)/shard_map/while/body/eval_jaxpr/ppermute | solution.py:12
  169.0 1.9 collective-permute-start
  170.9 1.9 bitcast_add_fusion.2
  172.8 7.2 %collective-permute-done = bf16[1024,128]{1,0:T(8,128)(2,1)} collective-permute-done((bf16[1024,128]{1,0:T(8,128)(2,1)S(1)}, bf16[1024,128]{1,0:T(8,128)(2,1)}, u32[]{:S(2)}, u32[]{:S(2)}) %collective-permute-start) | collective-permute-done | bytes 262176 | tf_op jit(solution)/shard_map/while/body/eval_jaxpr/ppermute | solution.py:12
  181.0 1.9 collective-permute-start
  182.9 1.9 bitcast_add_fusion.2
  184.8 6.3 %collective-permute-done = bf16[1024,128]{1,0:T(8,128)(2,1)} collective-permute-done((bf16[1024,128]{1,0:T(8,128)(2,1)S(1)}, bf16[1024,128]{1,0:T(8,128)(2,1)}, u32[]{:S(2)}, u32[]{:S(2)}) %collective-permute-start) | collective-permute-done | bytes 262176 | tf_op jit(solution)/shard_map/while/body/eval_jaxpr/ppermute | solution.py:12
  192.1 1.9 collective-permute-start
  194.0 1.9 bitcast_add_fusion.2
  195.9 5.7 %collective-permute-done = bf16[1024,128]{1,0:T(8,128)(2,1)} collective-permute-done((bf16[1024,128]{1,0:T(8,128)(2,1)S(1)}, bf16[1024,128]{1,0:T(8,128)(2,1)}, u32[]{:S(2)}, u32[]{:S(2)}) %collective-permute-start) | collective-permute-done | bytes 262176 | tf_op jit(solution)/shard_map/while/body/eval_jaxpr/ppermute | solution.py:12
  201.7 1.0 copy.29
  202.6 1.9 collective-permute-start
  204.6 1.9 bitcast_add_fusion.2
  206.4 5.7 %collective-permute-done = bf16[1024,128]{1,0:T(8,128)(2,1)} collective-permute-done((bf16[1024,128]{1,0:T(8,128)(2,1)S(1)}, bf16[1024,128]{1,0:T(8,128)(2,1)}, u32[]{:S(2)}, u32[]{:S(2)}) %collective-permute-start) | collective-permute-done | bytes 262176 | tf_op jit(solution)/shard_map/while/body/eval_jaxpr/ppermute | solution.py:12
  212.2 1.0 copy.29
  213.1 1.9 collective-permute-start
  215.1 1.9 bitcast_add_fusion.2
  217.0 5.7 %collective-permute-done = bf16[1024,128]{1,0:T(8,128)(2,1)} collective-permute-done((bf16[1024,128]{1,0:T(8,128)(2,1)S(1)}, bf16[1024,128]{1,0:T(8,128)(2,1)}, u32[]{:S(2)}, u32[]{:S(2)}) %collective-permute-start) | collective-permute-done | bytes 262176 | tf_op jit(solution)/shard_map/while/body/eval_jaxpr/ppermute | solution.py:12
  222.7 2.4 copy.12
  225.1 2.6 convolution_add_fusion
  227.7 2.3 copy.13
  230.0 2.6 copy.19
  233.0 114.2 %all-reduce.1 = bf16[8,128,6,128]{1,0,3,2:T(8,128)(2,1)} all-reduce(f32[8,128,6,128]{1,0,3,2:T(8,128)S(1)} %broadcast_multiply_fusion), channel_id=1, replica_groups=mesh['row'=16,'col'=4,'depth'=8] {'depth'}, use_global_device_ids=true, to_apply=%region_2.3 | all-reduce | flops 786432 | bytes 4718592 | tf_op jit(solution)/shard_map/psum | solution.py:54
  347.1 1.9 fusion.3
  (23 shorter events, 9.8 us)
Async XLA Ops:
  6.5 3.7 %copy-start = (s32[1,8]{1,0:T(1,128)S(1)}, s32[1,8]{1,0:T(1,128)}, u32[]{:S(2)}) copy-start(s32[1,8]{1,0:T(1,128)} %param.13) | copy-start | bytes 100
  6.5 45.1 %all-gather.2.cloned.1.call-start = ((), (), s32[]{:S(2)}) async-start(), calls=%async_computation | async-start | bytes 3932160 | tf_op jit(solution)/shard_map/all_gather | solution.py:30
  52.6 13.0 %collective-permute-start = (bf16[1024,128]{1,0:T(8,128)(2,1)S(1)}, bf16[1024,128]{1,0:T(8,128)(2,1)}, u32[]{:S(2)}, u32[]{:S(2)}) collective-permute-start(bf16[1024,128]{1,0:T(8,128)(2,1)S(1)} %copy.29), channel_id=1, source_target_pairs={{480,0},{0,32},{32,64},{64,96},{96,128},{128,160},{160,192},{192,2... | collective-permute-start | bytes 786440 | tf_op jit(solution)/shard_map/while/body/eval_jaxpr/ppermute | solution.py:12
  66.5 11.2 %collective-permute-start = (bf16[1024,128]{1,0:T(8,128)(2,1)S(1)}, bf16[1024,128]{1,0:T(8,128)(2,1)}, u32[]{:S(2)}, u32[]{:S(2)}) collective-permute-start(bf16[1024,128]{1,0:T(8,128)(2,1)S(1)} %copy.29), channel_id=1, source_target_pairs={{480,0},{0,32},{32,64},{64,96},{96,128},{128,160},{160,192},{192,2... | collective-permute-start | bytes 786440 | tf_op jit(solution)/shard_map/while/body/eval_jaxpr/ppermute | solution.py:12
  78.6 10.3 %collective-permute-start = (bf16[1024,128]{1,0:T(8,128)(2,1)S(1)}, bf16[1024,128]{1,0:T(8,128)(2,1)}, u32[]{:S(2)}, u32[]{:S(2)}) collective-permute-start(bf16[1024,128]{1,0:T(8,128)(2,1)S(1)} %copy.29), channel_id=1, source_target_pairs={{480,0},{0,32},{32,64},{64,96},{96,128},{128,160},{160,192},{192,2... | collective-permute-start | bytes 786440 | tf_op jit(solution)/shard_map/while/body/eval_jaxpr/ppermute | solution.py:12
  89.9 9.6 %collective-permute-start = (bf16[1024,128]{1,0:T(8,128)(2,1)S(1)}, bf16[1024,128]{1,0:T(8,128)(2,1)}, u32[]{:S(2)}, u32[]{:S(2)}) collective-permute-start(bf16[1024,128]{1,0:T(8,128)(2,1)S(1)} %copy.29), channel_id=1, source_target_pairs={{480,0},{0,32},{32,64},{64,96},{96,128},{128,160},{160,192},{192,2... | collective-permute-start | bytes 786440 | tf_op jit(solution)/shard_map/while/body/eval_jaxpr/ppermute | solution.py:12
  100.4 9.6 %collective-permute-start = (bf16[1024,128]{1,0:T(8,128)(2,1)S(1)}, bf16[1024,128]{1,0:T(8,128)(2,1)}, u32[]{:S(2)}, u32[]{:S(2)}) collective-permute-start(bf16[1024,128]{1,0:T(8,128)(2,1)S(1)} %copy.29), channel_id=1, source_target_pairs={{480,0},{0,32},{32,64},{64,96},{96,128},{128,160},{160,192},{192,2... | collective-permute-start | bytes 786440 | tf_op jit(solution)/shard_map/while/body/eval_jaxpr/ppermute | solution.py:12
  110.9 9.6 %collective-permute-start = (bf16[1024,128]{1,0:T(8,128)(2,1)S(1)}, bf16[1024,128]{1,0:T(8,128)(2,1)}, u32[]{:S(2)}, u32[]{:S(2)}) collective-permute-start(bf16[1024,128]{1,0:T(8,128)(2,1)S(1)} %copy.29), channel_id=1, source_target_pairs={{480,0},{0,32},{32,64},{64,96},{96,128},{128,160},{160,192},{192,2... | collective-permute-start | bytes 786440 | tf_op jit(solution)/shard_map/while/body/eval_jaxpr/ppermute | solution.py:12
  121.4 9.6 %collective-permute-start = (bf16[1024,128]{1,0:T(8,128)(2,1)S(1)}, bf16[1024,128]{1,0:T(8,128)(2,1)}, u32[]{:S(2)}, u32[]{:S(2)}) collective-permute-start(bf16[1024,128]{1,0:T(8,128)(2,1)S(1)} %copy.29), channel_id=1, source_target_pairs={{480,0},{0,32},{32,64},{64,96},{96,128},{128,160},{160,192},{192,2... | collective-permute-start | bytes 786440 | tf_op jit(solution)/shard_map/while/body/eval_jaxpr/ppermute | solution.py:12
  131.9 10.6 %collective-permute-start = (bf16[1024,128]{1,0:T(8,128)(2,1)S(1)}, bf16[1024,128]{1,0:T(8,128)(2,1)}, u32[]{:S(2)}, u32[]{:S(2)}) collective-permute-start(bf16[1024,128]{1,0:T(8,128)(2,1)S(1)} %copy.29), channel_id=1, source_target_pairs={{480,0},{0,32},{32,64},{64,96},{96,128},{128,160},{160,192},{192,2... | collective-permute-start | bytes 786440 | tf_op jit(solution)/shard_map/while/body/eval_jaxpr/ppermute | solution.py:12
  143.5 11.8 %collective-permute-start = (bf16[1024,128]{1,0:T(8,128)(2,1)S(1)}, bf16[1024,128]{1,0:T(8,128)(2,1)}, u32[]{:S(2)}, u32[]{:S(2)}) collective-permute-start(bf16[1024,128]{1,0:T(8,128)(2,1)S(1)} %copy.29), channel_id=1, source_target_pairs={{480,0},{0,32},{32,64},{64,96},{96,128},{128,160},{160,192},{192,2... | collective-permute-start | bytes 786440 | tf_op jit(solution)/shard_map/while/body/eval_jaxpr/ppermute | solution.py:12
  156.2 11.8 %collective-permute-start = (bf16[1024,128]{1,0:T(8,128)(2,1)S(1)}, bf16[1024,128]{1,0:T(8,128)(2,1)}, u32[]{:S(2)}, u32[]{:S(2)}) collective-permute-start(bf16[1024,128]{1,0:T(8,128)(2,1)S(1)} %copy.29), channel_id=1, source_target_pairs={{480,0},{0,32},{32,64},{64,96},{96,128},{128,160},{160,192},{192,2... | collective-permute-start | bytes 786440 | tf_op jit(solution)/shard_map/while/body/eval_jaxpr/ppermute | solution.py:12
  169.0 11.1 %collective-permute-start = (bf16[1024,128]{1,0:T(8,128)(2,1)S(1)}, bf16[1024,128]{1,0:T(8,128)(2,1)}, u32[]{:S(2)}, u32[]{:S(2)}) collective-permute-start(bf16[1024,128]{1,0:T(8,128)(2,1)S(1)} %copy.29), channel_id=1, source_target_pairs={{480,0},{0,32},{32,64},{64,96},{96,128},{128,160},{160,192},{192,2... | collective-permute-start | bytes 786440 | tf_op jit(solution)/shard_map/while/body/eval_jaxpr/ppermute | solution.py:12
  181.0 10.2 %collective-permute-start = (bf16[1024,128]{1,0:T(8,128)(2,1)S(1)}, bf16[1024,128]{1,0:T(8,128)(2,1)}, u32[]{:S(2)}, u32[]{:S(2)}) collective-permute-start(bf16[1024,128]{1,0:T(8,128)(2,1)S(1)} %copy.29), channel_id=1, source_target_pairs={{480,0},{0,32},{32,64},{64,96},{96,128},{128,160},{160,192},{192,2... | collective-permute-start | bytes 786440 | tf_op jit(solution)/shard_map/while/body/eval_jaxpr/ppermute | solution.py:12
  192.1 9.6 %collective-permute-start = (bf16[1024,128]{1,0:T(8,128)(2,1)S(1)}, bf16[1024,128]{1,0:T(8,128)(2,1)}, u32[]{:S(2)}, u32[]{:S(2)}) collective-permute-start(bf16[1024,128]{1,0:T(8,128)(2,1)S(1)} %copy.29), channel_id=1, source_target_pairs={{480,0},{0,32},{32,64},{64,96},{96,128},{128,160},{160,192},{192,2... | collective-permute-start | bytes 786440 | tf_op jit(solution)/shard_map/while/body/eval_jaxpr/ppermute | solution.py:12
  202.6 9.6 %collective-permute-start = (bf16[1024,128]{1,0:T(8,128)(2,1)S(1)}, bf16[1024,128]{1,0:T(8,128)(2,1)}, u32[]{:S(2)}, u32[]{:S(2)}) collective-permute-start(bf16[1024,128]{1,0:T(8,128)(2,1)S(1)} %copy.29), channel_id=1, source_target_pairs={{480,0},{0,32},{32,64},{64,96},{96,128},{128,160},{160,192},{192,2... | collective-permute-start | bytes 786440 | tf_op jit(solution)/shard_map/while/body/eval_jaxpr/ppermute | solution.py:12
  213.1 9.6 %collective-permute-start = (bf16[1024,128]{1,0:T(8,128)(2,1)S(1)}, bf16[1024,128]{1,0:T(8,128)(2,1)}, u32[]{:S(2)}, u32[]{:S(2)}) collective-permute-start(bf16[1024,128]{1,0:T(8,128)(2,1)S(1)} %copy.29), channel_id=1, source_target_pairs={{480,0},{0,32},{32,64},{64,96},{96,128},{128,160},{160,192},{192,2... | collective-permute-start | bytes 786440 | tf_op jit(solution)/shard_map/while/body/eval_jaxpr/ppermute | solution.py:12
Sparse Core Ops, SparseCore 0:
  9.5 42.0 all-gather.1
where the time goes:
time: 358 us; the launch traced here: 357 us
  waiting for transfers between devices  134 us (37%)
  blocking collectives  114 us (32%)
  matrix products  30.7 us (9%)
  starting transfers between devices  30.4 us (8%)
  local copies, waits for them, and re-layouts  23.3 us (7%)
  between operations  15.4 us (4%)
  other arithmetic  8.19 us (2%)
    psum x1, blocking collectives, per_device(): summed = lax.psum(filtered, 'depth')  114 us
    ppermute x15, waiting for transfers between devices, from_behind(): return lax.ppermute(block, axis, route)  97.7 us
    all_gather x1, waiting for transfers between devices, per_device(): sign_whole = lax.all_gather(sign_kept, 'col', axis=0, tiled=True)  36.3 us
    ppermute x15, starting transfers between devices, from_behind(): return lax.ppermute(block, axis, route)  30.4 us
    dot_general x15, matrix products, advance(): jnp.dot(moving, sign_piece, preferred_element_type=jnp.float32)  28.1 us
    while x15, local copies, waits for them, and re-layouts  14.3 us
  transfers between devices with their start and end apart: 16, of which 16 were waited for; matrix products, arithmetic and copies ran while one was open for 9% of the time, Pallas kernels for 0%

commit v1 on v0

--- a/solution.py
+++ b/solution.py
@@ -27,7 +27,9 @@
         local_groups, sign_inner, 1, col_blocks, 1
     )
     sign_kept = sign_kept.reshape(local_groups, 1, sign_inner * BS, col_blocks * BS)
-    sign_whole = lax.all_gather(sign_kept, "col", axis=0, tiled=True)
+    sign_whole = jnp.concatenate(
+        lax.all_to_all(jnp.stack([sign_kept] * lax.axis_size("col")), "col", 0, 0), axis=0
+    )
     row_count = lax.axis_size("row")
     start_sum = jnp.zeros((row_blocks * BS, col_blocks * BS), jnp.float32)
     row_index = lax.axis_index("row")

time: 358 us -> 349 us (0.975)
  between operations: 15.4 us -> 2.02 us
  starting transfers between devices: 30.4 us -> 39.3 us
  waiting for transfers between devices: 134 us -> 130 us
    all_gather x1 -> x0, waiting for transfers between devices: 36.3 us -> none  [per_device(): sign_whole = lax.all_gather(sign_kept, 'col', axis=0, tiled=True)]
    all_to_all x0 -> x1, waiting for transfers between devices: none -> 31.8 us  [per_device(): lax.all_to_all(jnp.stack([sign_kept] * lax.axis_size('col')), 'col', 0, 0)]
    all_to_all x0 -> x1, starting transfers between devices: none -> 10.6 us  [per_device(): lax.all_to_all(jnp.stack([sign_kept] * lax.axis_size('col')), 'col', 0, 0)]
where the time goes in v1:
time: 349 us; the launch traced here: 347 us
  waiting for transfers between devices  130 us (37%)
  blocking collectives  114 us (33%)
  starting transfers between devices  39.3 us (11%)
  matrix products  30.7 us (9%)
  local copies, waits for them, and re-layouts  25.3 us (7%)
  other arithmetic  5.23 us (1%)
    psum x1, blocking collectives, per_device(): summed = lax.psum(filtered, 'depth')  114 us
    ppermute x15, waiting for transfers between devices, from_behind(): return lax.ppermute(block, axis, route)  98 us
    all_to_all x1, waiting for transfers between devices, per_device(): lax.all_to_all(jnp.stack([sign_kept] * lax.axis_size('col')), 'col', 0, 0)  31.8 us
    ppermute x15, starting transfers between devices, from_behind(): return lax.ppermute(block, axis, route)  28.6 us
    dot_general x15, matrix products, advance(): jnp.dot(moving, sign_piece, preferred_element_type=jnp.float32)  28.1 us
    while x15, local copies, waits for them, and re-layouts  14.3 us
    all_to_all x1, starting transfers between devices, per_device(): lax.all_to_all(jnp.stack([sign_kept] * lax.axis_size('col')), 'col', 0, 0)  10.6 us
  transfers between devices with their start and end apart: 16, of which 16 were waited for; matrix products, arithmetic and copies ran while one was open for 9% of the time, Pallas kernels for 0%

profile of v1, /device:TPU:4, one launch (start us, length us, event | category | flops | bytes accessed | tf_op | source)
XLA Modules:
  0.0 347.3 jit_solution(16675154711232431685)
XLA Ops:
  0.8 1.2 multiply_bitcast_fusion
  2.0 2.0 stack.3
  4.0 10.6 %all-to-all-start = ((bf16[4,4,1,128,768]{4,3,1,2,0:T(8,128)(2,1)}), bf16[4,4,1,128,768]{4,3,1,2,0:T(8,128)(2,1)}, u32[]{:S(2)}, u32[]{:S(2)}) async-start(bf16[4,4,1,128,768]{4,3,1,2,0:T(8,128)(2,1)} %stack.3), calls=%async_computation | async-start | bytes 6291456 | tf_op jit(solution)/shard_map/all_to_all | solution.py:31
  18.2 31.8 %all-to-all-done = bf16[4,4,1,128,768]{4,3,1,2,0:T(8,128)(2,1)} async-done(((bf16[4,4,1,128,768]{4,3,1,2,0:T(8,128)(2,1)}), bf16[4,4,1,128,768]{4,3,1,2,0:T(8,128)(2,1)}, u32[]{:S(2)}, u32[]{:S(2)}) %all-to-all-start) | async-done | bytes 3145760 | tf_op jit(solution)/shard_map/all_to_all | solution.py:31
  50.0 169.7 %while.19 = (s32[]{:T(128)}, f32[1024,768]{0,1:T(8,128)S(1)}, bf16[1024,128]{1,0:T(8,128)(2,1)}, s32[]{:T(128)}, bf16[16,1,128,768]{3,2,1,0:T(8,128)(2,1)}, /*index=5*/s32[]{:T(128)}, s32[]{:T(128)}, s32[]{:T(128)}, s32[]{:T(128)}) while((s32[]{:T(128)}, f32[1024,768]{0,1:T(8,128)S(1)}, bf16[1024,128]{1,0:T(8,128)(2,1)}, ...), condition=%wide.region_1.2_spmd.clone, body=%wide.region_0.1_spmd.clone.sunk | while | flops 202899472 | bytes 8323374 | solution.py:45
  50.0 1.0 copy.30
  50.9 1.9 collective-permute-start
  52.9 1.9 bitcast_add_fusion.2
  54.8 8.7 %collective-permute-done = bf16[1024,128]{1,0:T(8,128)(2,1)} collective-permute-done((bf16[1024,128]{1,0:T(8,128)(2,1)S(1)}, bf16[1024,128]{1,0:T(8,128)(2,1)}, u32[]{:S(2)}, u32[]{:S(2)}) %collective-permute-start) | collective-permute-done | bytes 262176 | tf_op jit(solution)/shard_map/while/body/eval_jaxpr/ppermute | solution.py:12
  63.4 1.0 copy.30
  64.4 1.9 collective-permute-start
  66.3 1.9 bitcast_add_fusion.2
  68.2 6.9 %collective-permute-done = bf16[1024,128]{1,0:T(8,128)(2,1)} collective-permute-done((bf16[1024,128]{1,0:T(8,128)(2,1)S(1)}, bf16[1024,128]{1,0:T(8,128)(2,1)}, u32[]{:S(2)}, u32[]{:S(2)}) %collective-permute-start) | collective-permute-done | bytes 262176 | tf_op jit(solution)/shard_map/while/body/eval_jaxpr/ppermute | solution.py:12
  75.1 1.0 copy.30
  76.1 1.9 collective-permute-start
  78.0 1.9 bitcast_add_fusion.2
  79.9 6.0 %collective-permute-done = bf16[1024,128]{1,0:T(8,128)(2,1)} collective-permute-done((bf16[1024,128]{1,0:T(8,128)(2,1)S(1)}, bf16[1024,128]{1,0:T(8,128)(2,1)}, u32[]{:S(2)}, u32[]{:S(2)}) %collective-permute-start) | collective-permute-done | bytes 262176 | tf_op jit(solution)/shard_map/while/body/eval_jaxpr/ppermute | solution.py:12
  86.9 1.9 collective-permute-start
  88.8 1.9 bitcast_add_fusion.2
  90.7 5.7 %collective-permute-done = bf16[1024,128]{1,0:T(8,128)(2,1)} collective-permute-done((bf16[1024,128]{1,0:T(8,128)(2,1)S(1)}, bf16[1024,128]{1,0:T(8,128)(2,1)}, u32[]{:S(2)}, u32[]{:S(2)}) %collective-permute-start) | collective-permute-done | bytes 262176 | tf_op jit(solution)/shard_map/while/body/eval_jaxpr/ppermute | solution.py:12
  96.5 1.0 copy.30
  97.4 1.9 collective-permute-start
  99.4 1.9 bitcast_add_fusion.2
  101.2 5.7 %collective-permute-done = bf16[1024,128]{1,0:T(8,128)(2,1)} collective-permute-done((bf16[1024,128]{1,0:T(8,128)(2,1)S(1)}, bf16[1024,128]{1,0:T(8,128)(2,1)}, u32[]{:S(2)}, u32[]{:S(2)}) %collective-permute-start) | collective-permute-done | bytes 262176 | tf_op jit(solution)/shard_map/while/body/eval_jaxpr/ppermute | solution.py:12
  107.0 1.0 copy.30
  107.9 1.9 collective-permute-start
  109.9 1.9 bitcast_add_fusion.2
  111.8 5.7 %collective-permute-done = bf16[1024,128]{1,0:T(8,128)(2,1)} collective-permute-done((bf16[1024,128]{1,0:T(8,128)(2,1)S(1)}, bf16[1024,128]{1,0:T(8,128)(2,1)}, u32[]{:S(2)}, u32[]{:S(2)}) %collective-permute-start) | collective-permute-done | bytes 262176 | tf_op jit(solution)/shard_map/while/body/eval_jaxpr/ppermute | solution.py:12
  118.5 1.9 collective-permute-start
  120.4 1.9 bitcast_add_fusion.2
  122.3 6.0 %collective-permute-done = bf16[1024,128]{1,0:T(8,128)(2,1)} collective-permute-done((bf16[1024,128]{1,0:T(8,128)(2,1)S(1)}, bf16[1024,128]{1,0:T(8,128)(2,1)}, u32[]{:S(2)}, u32[]{:S(2)}) %collective-permute-start) | collective-permute-done | bytes 262176 | tf_op jit(solution)/shard_map/while/body/eval_jaxpr/ppermute | solution.py:12
  128.3 1.0 copy.30
  129.2 1.9 collective-permute-start
  131.2 1.9 bitcast_add_fusion.2
  133.1 7.1 %collective-permute-done = bf16[1024,128]{1,0:T(8,128)(2,1)} collective-permute-done((bf16[1024,128]{1,0:T(8,128)(2,1)S(1)}, bf16[1024,128]{1,0:T(8,128)(2,1)}, u32[]{:S(2)}, u32[]{:S(2)}) %collective-permute-start) | collective-permute-done | bytes 262176 | tf_op jit(solution)/shard_map/while/body/eval_jaxpr/ppermute | solution.py:12
  141.1 1.9 collective-permute-start
  143.1 1.9 bitcast_add_fusion.2
  144.9 8.3 %collective-permute-done = bf16[1024,128]{1,0:T(8,128)(2,1)} collective-permute-done((bf16[1024,128]{1,0:T(8,128)(2,1)S(1)}, bf16[1024,128]{1,0:T(8,128)(2,1)}, u32[]{:S(2)}, u32[]{:S(2)}) %collective-permute-start) | collective-permute-done | bytes 262176 | tf_op jit(solution)/shard_map/while/body/eval_jaxpr/ppermute | solution.py:12
  154.2 1.9 collective-permute-start
  156.1 1.9 bitcast_add_fusion.2
  158.0 7.7 %collective-permute-done = bf16[1024,128]{1,0:T(8,128)(2,1)} collective-permute-done((bf16[1024,128]{1,0:T(8,128)(2,1)S(1)}, bf16[1024,128]{1,0:T(8,128)(2,1)}, u32[]{:S(2)}, u32[]{:S(2)}) %collective-permute-start) | collective-permute-done | bytes 262176 | tf_op jit(solution)/shard_map/while/body/eval_jaxpr/ppermute | solution.py:12
  166.6 1.9 collective-permute-start
  168.6 1.9 bitcast_add_fusion.2
  170.5 6.9 %collective-permute-done = bf16[1024,128]{1,0:T(8,128)(2,1)} collective-permute-done((bf16[1024,128]{1,0:T(8,128)(2,1)S(1)}, bf16[1024,128]{1,0:T(8,128)(2,1)}, u32[]{:S(2)}, u32[]{:S(2)}) %collective-permute-start) | collective-permute-done | bytes 262176 | tf_op jit(solution)/shard_map/while/body/eval_jaxpr/ppermute | solution.py:12
  177.3 1.0 copy.30
  178.3 1.9 collective-permute-start
  180.2 1.9 bitcast_add_fusion.2
  182.1 6.0 %collective-permute-done = bf16[1024,128]{1,0:T(8,128)(2,1)} collective-permute-done((bf16[1024,128]{1,0:T(8,128)(2,1)S(1)}, bf16[1024,128]{1,0:T(8,128)(2,1)}, u32[]{:S(2)}, u32[]{:S(2)}) %collective-permute-start) | collective-permute-done | bytes 262176 | tf_op jit(solution)/shard_map/while/body/eval_jaxpr/ppermute | solution.py:12
  189.0 1.9 collective-permute-start
  191.0 1.9 bitcast_add_fusion.2
  192.8 5.7 %collective-permute-done = bf16[1024,128]{1,0:T(8,128)(2,1)} collective-permute-done((bf16[1024,128]{1,0:T(8,128)(2,1)S(1)}, bf16[1024,128]{1,0:T(8,128)(2,1)}, u32[]{:S(2)}, u32[]{:S(2)}) %collective-permute-start) | collective-permute-done | bytes 262176 | tf_op jit(solution)/shard_map/while/body/eval_jaxpr/ppermute | solution.py:12
  198.6 1.0 copy.30
  199.5 1.9 collective-permute-start
  201.5 1.9 bitcast_add_fusion.2
  203.4 5.7 %collective-permute-done = bf16[1024,128]{1,0:T(8,128)(2,1)} collective-permute-done((bf16[1024,128]{1,0:T(8,128)(2,1)S(1)}, bf16[1024,128]{1,0:T(8,128)(2,1)}, u32[]{:S(2)}, u32[]{:S(2)}) %collective-permute-start) | collective-permute-done | bytes 262176 | tf_op jit(solution)/shard_map/while/body/eval_jaxpr/ppermute | solution.py:12
  210.1 1.9 collective-permute-start
  212.0 1.9 bitcast_add_fusion.2
  213.9 5.7 %collective-permute-done = bf16[1024,128]{1,0:T(8,128)(2,1)} collective-permute-done((bf16[1024,128]{1,0:T(8,128)(2,1)S(1)}, bf16[1024,128]{1,0:T(8,128)(2,1)}, u32[]{:S(2)}, u32[]{:S(2)}) %collective-permute-start) | collective-permute-done | bytes 262176 | tf_op jit(solution)/shard_map/while/body/eval_jaxpr/ppermute | solution.py:12
  219.6 2.4 copy.13
  222.0 2.6 convolution_add_fusion
  224.6 2.4 copy.14
  227.0 2.6 copy.20
  229.6 1.9 broadcast_multiply_fusion
  231.5 114.4 %all-reduce.1 = bf16[8,128,6,128]{1,0,3,2:T(8,128)(2,1)S(1)} all-reduce(f32[8,128,6,128]{1,0,3,2:T(8,128)} %broadcast_multiply_fusion), channel_id=1, replica_groups=mesh['row'=16,'col'=4,'depth'=8] {'depth'}, use_global_device_ids=true, to_apply=%region_2.3 | all-reduce | flops 786432 | bytes 4718592 | tf_op jit(solution)/shard_map/psum | solution.py:56
  (29 shorter events, 10.5 us)
Async XLA Ops:
  0.0 14.7 %copy-start = (s32[1,8]{1,0:T(1,128)S(1)}, s32[1,8]{1,0:T(1,128)}, u32[]{:S(2)}) copy-start(s32[1,8]{1,0:T(1,128)} %param.13) | copy-start | bytes 100
  4.0 10.6 %copy-start.2 = (s32[8,6]{1,0:T(8,128)S(1)}, s32[8,6]{1,0:T(8,128)}, u32[]{:S(2)}) copy-start(s32[8,6]{1,0:T(8,128)} %param.12) | copy-start | bytes 580
  4.0 13.3 %copy-start.3 = (s32[8,1]{0,1:T(1,128)S(1)}, s32[8,1]{0,1:T(1,128)}, u32[]{:S(2)}) copy-start(s32[8,1]{0,1:T(1,128)} %param.10) | copy-start | bytes 100
  4.0 13.4 %copy-start.1 = (bf16[1024,128]{1,0:T(8,128)(2,1)S(1)}, bf16[1024,128]{1,0:T(8,128)(2,1)}, u32[]{:S(2)}) copy-start(bf16[1024,128]{1,0:T(8,128)(2,1)} %param.8) | copy-start | bytes 786436
  4.0 46.0 %all-to-all-start = ((bf16[4,4,1,128,768]{4,3,1,2,0:T(8,128)(2,1)}), bf16[4,4,1,128,768]{4,3,1,2,0:T(8,128)(2,1)}, u32[]{:S(2)}, u32[]{:S(2)}) async-start(bf16[4,4,1,128,768]{4,3,1,2,0:T(8,128)(2,1)} %stack.3), calls=%async_computation | async-start | bytes 6291456 | tf_op jit(solution)/shard_map/all_to_all | solution.py:31
  50.9 12.5 %collective-permute-start = (bf16[1024,128]{1,0:T(8,128)(2,1)S(1)}, bf16[1024,128]{1,0:T(8,128)(2,1)}, u32[]{:S(2)}, u32[]{:S(2)}) collective-permute-start(bf16[1024,128]{1,0:T(8,128)(2,1)S(1)} %copy.30), channel_id=1, source_target_pairs={{480,0},{0,32},{32,64},{64,96},{96,128},{128,160},{160,192},{192,2... | collective-permute-start | bytes 786440 | tf_op jit(solution)/shard_map/while/body/eval_jaxpr/ppermute | solution.py:12
  64.4 10.8 %collective-permute-start = (bf16[1024,128]{1,0:T(8,128)(2,1)S(1)}, bf16[1024,128]{1,0:T(8,128)(2,1)}, u32[]{:S(2)}, u32[]{:S(2)}) collective-permute-start(bf16[1024,128]{1,0:T(8,128)(2,1)S(1)} %copy.30), channel_id=1, source_target_pairs={{480,0},{0,32},{32,64},{64,96},{96,128},{128,160},{160,192},{192,2... | collective-permute-start | bytes 786440 | tf_op jit(solution)/shard_map/while/body/eval_jaxpr/ppermute | solution.py:12
  76.1 9.8 %collective-permute-start = (bf16[1024,128]{1,0:T(8,128)(2,1)S(1)}, bf16[1024,128]{1,0:T(8,128)(2,1)}, u32[]{:S(2)}, u32[]{:S(2)}) collective-permute-start(bf16[1024,128]{1,0:T(8,128)(2,1)S(1)} %copy.30), channel_id=1, source_target_pairs={{480,0},{0,32},{32,64},{64,96},{96,128},{128,160},{160,192},{192,2... | collective-permute-start | bytes 786440 | tf_op jit(solution)/shard_map/while/body/eval_jaxpr/ppermute | solution.py:12
  86.9 9.6 %collective-permute-start = (bf16[1024,128]{1,0:T(8,128)(2,1)S(1)}, bf16[1024,128]{1,0:T(8,128)(2,1)}, u32[]{:S(2)}, u32[]{:S(2)}) collective-permute-start(bf16[1024,128]{1,0:T(8,128)(2,1)S(1)} %copy.30), channel_id=1, source_target_pairs={{480,0},{0,32},{32,64},{64,96},{96,128},{128,160},{160,192},{192,2... | collective-permute-start | bytes 786440 | tf_op jit(solution)/shard_map/while/body/eval_jaxpr/ppermute | solution.py:12
  97.4 9.6 %collective-permute-start = (bf16[1024,128]{1,0:T(8,128)(2,1)S(1)}, bf16[1024,128]{1,0:T(8,128)(2,1)}, u32[]{:S(2)}, u32[]{:S(2)}) collective-permute-start(bf16[1024,128]{1,0:T(8,128)(2,1)S(1)} %copy.30), channel_id=1, source_target_pairs={{480,0},{0,32},{32,64},{64,96},{96,128},{128,160},{160,192},{192,2... | collective-permute-start | bytes 786440 | tf_op jit(solution)/shard_map/while/body/eval_jaxpr/ppermute | solution.py:12
  107.9 9.6 %collective-permute-start = (bf16[1024,128]{1,0:T(8,128)(2,1)S(1)}, bf16[1024,128]{1,0:T(8,128)(2,1)}, u32[]{:S(2)}, u32[]{:S(2)}) collective-permute-start(bf16[1024,128]{1,0:T(8,128)(2,1)S(1)} %copy.30), channel_id=1, source_target_pairs={{480,0},{0,32},{32,64},{64,96},{96,128},{128,160},{160,192},{192,2... | collective-permute-start | bytes 786440 | tf_op jit(solution)/shard_map/while/body/eval_jaxpr/ppermute | solution.py:12
  118.5 9.8 %collective-permute-start = (bf16[1024,128]{1,0:T(8,128)(2,1)S(1)}, bf16[1024,128]{1,0:T(8,128)(2,1)}, u32[]{:S(2)}, u32[]{:S(2)}) collective-permute-start(bf16[1024,128]{1,0:T(8,128)(2,1)S(1)} %copy.30), channel_id=1, source_target_pairs={{480,0},{0,32},{32,64},{64,96},{96,128},{128,160},{160,192},{192,2... | collective-permute-start | bytes 786440 | tf_op jit(solution)/shard_map/while/body/eval_jaxpr/ppermute | solution.py:12
  129.2 10.9 %collective-permute-start = (bf16[1024,128]{1,0:T(8,128)(2,1)S(1)}, bf16[1024,128]{1,0:T(8,128)(2,1)}, u32[]{:S(2)}, u32[]{:S(2)}) collective-permute-start(bf16[1024,128]{1,0:T(8,128)(2,1)S(1)} %copy.30), channel_id=1, source_target_pairs={{480,0},{0,32},{32,64},{64,96},{96,128},{128,160},{160,192},{192,2... | collective-permute-start | bytes 786440 | tf_op jit(solution)/shard_map/while/body/eval_jaxpr/ppermute | solution.py:12
  141.1 12.1 %collective-permute-start = (bf16[1024,128]{1,0:T(8,128)(2,1)S(1)}, bf16[1024,128]{1,0:T(8,128)(2,1)}, u32[]{:S(2)}, u32[]{:S(2)}) collective-permute-start(bf16[1024,128]{1,0:T(8,128)(2,1)S(1)} %copy.30), channel_id=1, source_target_pairs={{480,0},{0,32},{32,64},{64,96},{96,128},{128,160},{160,192},{192,2... | collective-permute-start | bytes 786440 | tf_op jit(solution)/shard_map/while/body/eval_jaxpr/ppermute | solution.py:12
  154.2 11.5 %collective-permute-start = (bf16[1024,128]{1,0:T(8,128)(2,1)S(1)}, bf16[1024,128]{1,0:T(8,128)(2,1)}, u32[]{:S(2)}, u32[]{:S(2)}) collective-permute-start(bf16[1024,128]{1,0:T(8,128)(2,1)S(1)} %copy.30), channel_id=1, source_target_pairs={{480,0},{0,32},{32,64},{64,96},{96,128},{128,160},{160,192},{192,2... | collective-permute-start | bytes 786440 | tf_op jit(solution)/shard_map/while/body/eval_jaxpr/ppermute | solution.py:12
  166.6 10.7 %collective-permute-start = (bf16[1024,128]{1,0:T(8,128)(2,1)S(1)}, bf16[1024,128]{1,0:T(8,128)(2,1)}, u32[]{:S(2)}, u32[]{:S(2)}) collective-permute-start(bf16[1024,128]{1,0:T(8,128)(2,1)S(1)} %copy.30), channel_id=1, source_target_pairs={{480,0},{0,32},{32,64},{64,96},{96,128},{128,160},{160,192},{192,2... | collective-permute-start | bytes 786440 | tf_op jit(solution)/shard_map/while/body/eval_jaxpr/ppermute | solution.py:12
  178.3 9.8 %collective-permute-start = (bf16[1024,128]{1,0:T(8,128)(2,1)S(1)}, bf16[1024,128]{1,0:T(8,128)(2,1)}, u32[]{:S(2)}, u32[]{:S(2)}) collective-permute-start(bf16[1024,128]{1,0:T(8,128)(2,1)S(1)} %copy.30), channel_id=1, source_target_pairs={{480,0},{0,32},{32,64},{64,96},{96,128},{128,160},{160,192},{192,2... | collective-permute-start | bytes 786440 | tf_op jit(solution)/shard_map/while/body/eval_jaxpr/ppermute | solution.py:12
  189.0 9.6 %collective-permute-start = (bf16[1024,128]{1,0:T(8,128)(2,1)S(1)}, bf16[1024,128]{1,0:T(8,128)(2,1)}, u32[]{:S(2)}, u32[]{:S(2)}) collective-permute-start(bf16[1024,128]{1,0:T(8,128)(2,1)S(1)} %copy.30), channel_id=1, source_target_pairs={{480,0},{0,32},{32,64},{64,96},{96,128},{128,160},{160,192},{192,2... | collective-permute-start | bytes 786440 | tf_op jit(solution)/shard_map/while/body/eval_jaxpr/ppermute | solution.py:12
  199.5 9.6 %collective-permute-start = (bf16[1024,128]{1,0:T(8,128)(2,1)S(1)}, bf16[1024,128]{1,0:T(8,128)(2,1)}, u32[]{:S(2)}, u32[]{:S(2)}) collective-permute-start(bf16[1024,128]{1,0:T(8,128)(2,1)S(1)} %copy.30), channel_id=1, source_target_pairs={{480,0},{0,32},{32,64},{64,96},{96,128},{128,160},{160,192},{192,2... | collective-permute-start | bytes 786440 | tf_op jit(solution)/shard_map/while/body/eval_jaxpr/ppermute | solution.py:12
  210.1 9.6 %collective-permute-start = (bf16[1024,128]{1,0:T(8,128)(2,1)S(1)}, bf16[1024,128]{1,0:T(8,128)(2,1)}, u32[]{:S(2)}, u32[]{:S(2)}) collective-permute-start(bf16[1024,128]{1,0:T(8,128)(2,1)S(1)} %copy.30), channel_id=1, source_target_pairs={{480,0},{0,32},{32,64},{64,96},{96,128},{128,160},{160,192},{192,2... | collective-permute-start | bytes 786440 | tf_op jit(solution)/shard_map/while/body/eval_jaxpr/ppermute | solution.py:12
